TPU v7x, 32 devices: a whole 2x2x4 slice. The times are simulated.
32 devices in a mesh: ctx: 4 (over x, core), ep: 8 (over z, y).
Axes of the slice: x: 2, y: 2, z: 4, core: 2. Of those that a mesh axis runs over, the one named last changes fastest.
Arguments:
- query_latent: bfloat16 [1, 512, 128, 512], P(None, 'ctx', 'ep'), may hold values from -6 to 6
- query_rope: bfloat16 [1, 128, 64, 512], P(None, 'ep', None, 'ctx'), may hold values from -12 to 12
- key_latent: bfloat16 [1, 512, 512], P(None, 'ctx'), may hold values from -6 to 6
- key_rope: bfloat16 [1, 64, 512], P(None, None, 'ctx'), may hold values from -14 to 14
- output_grad: bfloat16 [1, 512, 128, 512], P(None, 'ctx', 'ep'), may hold values from -6 to 6
Outputs:
- attended: bfloat16 [1, 512, 128, 512], P(None, 'ctx', 'ep')
- query_latent_grad: bfloat16 [1, 512, 128, 512], P(None, 'ctx', 'ep')
- query_rope_grad: bfloat16 [1, 128, 64, 512], P(None, 'ep', None, 'ctx')
- key_latent_grad: bfloat16 [1, 512, 512], P(None, 'ctx')
- key_rope_grad: bfloat16 [1, 64, 512], P(None, None, 'ctx')
All inputs are finite; a program needn't handle non-finite values.
Results may differ from a plain program's by a relative error of at most 0.018.
Values may be sent and summed in bfloat16 or wider, within the bound.
No kernel may reach another device: no remote copies, remote signals or barrier semaphores. Data moves between devices by JAX's collectives and lax.ppermute only.
A program may use at most 64 MiB of HBM per device.

v0:
```python
import jax
import jax.numpy as jnp
from jax import lax
from jax.sharding import PartitionSpec as P

scale_factor = 192.0 ** (-0.5)


def causal_reduce_ctx(blocks, n_ctx):
    here = lax.axis_index("ctx")
    total = jnp.take(blocks, here, axis=0).astype(jnp.float32)
    for shift in range(1, n_ctx):
        sent = jnp.take(blocks, jnp.maximum(here - shift, 0), axis=0)
        got = lax.ppermute(sent, "ctx", [(i, i - shift) for i in range(shift, n_ctx)])
        total = total + got.astype(jnp.float32)
    return total


def butterfly_sum_ep(total, n_ep):
    if n_ep & n_ep - 1:
        return lax.psum(total.astype(jnp.bfloat16), "ep").astype(jnp.float32)
    bit = 1
    while bit < n_ep:
        mine = total.astype(jnp.bfloat16)
        theirs = lax.ppermute(mine, "ep", [(i, i ^ bit) for i in range(n_ep)])
        total = mine.astype(jnp.float32) + theirs.astype(jnp.float32)
        bit *= 2
    return total


def body(query_latent, query_rope, key_latent, key_rope, output_grad):
    n_ctx = lax.axis_size("ctx")
    n_ep = lax.axis_size("ep")
    block_len = query_latent.shape[1]
    kvr = key_latent.shape[2]
    local_keys = jnp.concatenate([key_latent[0], key_rope[0].T], axis=1)
    whole_keys = lax.all_gather(local_keys, "ctx", axis=0, tiled=True)
    whole_latent = whole_keys[None, :, :kvr]
    whole_rope = whole_keys[:, kvr:].T[None]
    length = whole_latent.shape[1]
    offset = lax.axis_index("ctx") * block_len
    query_place = offset + jnp.arange(block_len, dtype=jnp.int32)
    allowed = jnp.arange(length, dtype=jnp.int32)[None, :] <= query_place[:, None]
    scores = jnp.einsum(
        "sthd,sjd->shtj", query_latent, whole_latent, preferred_element_type=jnp.float32
    )
    scores = scores + jnp.einsum(
        "shdt,sdj->shtj", query_rope, whole_rope, preferred_element_type=jnp.float32
    )
    scores = jnp.where(allowed, scores * scale_factor, jnp.float32(-1e30))
    row_max = jnp.max(scores, axis=-1, keepdims=True)
    powers = jnp.exp(scores - row_max)
    weights = powers / jnp.sum(powers, axis=-1, keepdims=True)
    rounded_weights = weights.astype(jnp.bfloat16)
    attended = jnp.einsum(
        "shtj,sjd->sthd", rounded_weights, whole_latent, preferred_element_type=jnp.float32
    ).astype(jnp.bfloat16)
    row_dots = jnp.einsum(
        "sthd,sthd->sht", output_grad, attended, preferred_element_type=jnp.float32
    )
    weight_grad = jnp.einsum(
        "sthd,sjd->shtj", output_grad, whole_latent, preferred_element_type=jnp.float32
    )
    score_grad = (weights * (weight_grad - row_dots[..., None])).astype(jnp.bfloat16)
    latent_qgrad = (
        scale_factor
        * jnp.einsum("shtj,sjd->sthd", score_grad, whole_latent, preferred_element_type=jnp.float32)
    ).astype(jnp.bfloat16)
    rope_qgrad = (
        scale_factor
        * jnp.einsum("shtj,sdj->shdt", score_grad, whole_rope, preferred_element_type=jnp.float32)
    ).astype(jnp.bfloat16)
    latent_term = scale_factor * jnp.einsum(
        "shtj,sthd->jd", score_grad, query_latent, preferred_element_type=jnp.float32
    )
    latent_term = latent_term + jnp.einsum(
        "shtj,sthd->jd", rounded_weights, output_grad, preferred_element_type=jnp.float32
    )
    rope_term = scale_factor * jnp.einsum(
        "shtj,shdt->jd", score_grad, query_rope, preferred_element_type=jnp.float32
    )
    terms = jnp.concatenate([latent_term, rope_term], axis=1).astype(jnp.bfloat16)
    total = causal_reduce_ctx(terms.reshape(n_ctx, block_len, -1), n_ctx)
    total = butterfly_sum_ep(total, n_ep).astype(jnp.bfloat16)
    latent_kgrad = total[None, :, :kvr]
    rope_kgrad = total[:, kvr:].T[None]
    return (attended, latent_qgrad, rope_qgrad, latent_kgrad, rope_kgrad)


def solution(mesh):
    placed = (
        P(None, "ctx", "ep", None),
        P(None, "ep", None, "ctx"),
        P(None, "ctx", None),
        P(None, None, "ctx"),
        P(None, "ctx", "ep", None),
    )
    return jax.shard_map(
        body,
        mesh=mesh,
        in_specs=placed,
        out_specs=(
            P(None, "ctx", "ep", None),
            P(None, "ctx", "ep", None),
            P(None, "ep", None, "ctx"),
            P(None, "ctx", None),
            P(None, None, "ctx"),
        ),
        check_vma=False,
    )
```

profile of v0, /device:TPU:0, one launch (start us, length us, event | category | flops | bytes accessed | tf_op | source)
XLA Modules:
  0.0 93.7 jit_solution(13140443794704222318)
XLA Ops:
  0.6 0.0 copy-start
  0.6 1.0 %copy.27 = bf16[1,64,128]{1,2,0:T(8,128)(2,1)S(1)} copy(bf16[1,64,128]{2,1,0:T(8,128)(2,1)} %param.10) | data formatting | bytes 32768 | tf_op args[3]
  1.6 0.9 pad_maximum_fusion
  2.6 9.3 %all_gather.3 = bf16[512,576]{1,0:T(8,128)(2,1)S(1)} all-gather(bf16[128,576]{1,0:T(8,128)(2,1)S(1)} %pad_maximum_fusion), channel_id=1, replica_groups=mesh['ctx'=4,'ep'=8] {'ctx'}, dimensions={0}, use_global_device_ids=true | all-gather | bytes 737280 | tf_op jit(solution)/shard_map/all_gather | solution.py:37
  11.9 0.1 iota_compare_fusion
  11.9 0.0 copy-done
  12.0 0.0 copy-start.4
  12.0 2.8 %fusion.23 = f32[512,128,16]{1,0,2:T(8,128)S(1)} fusion(bf16[128,16,512]{2,1,0:T(8,128)(2,1)S(1)} %bitcast.145, bf16[512,576]{1,0:T(8,128)(2,1)S(1)} %all_gather.3), kind=kOutput, calls=%fused_computation.27 | convolution fusion | flops 1073741824 | bytes 6815744 | tf_op jit(solution)/shard_map/sthd,sjd->shtj/dot_general | solution.py:44
  14.8 0.0 copy-done.4
  14.8 0.9 fusion.88
  15.7 0.0 copy-start.1
  15.7 0.6 fusion.5
  16.3 4.1 %bitcast_convert_fusion = (f32[16,128,512]{1,2,0:T(8,128)}, bf16[512,16,128]{2,0,1:T(8,128)(2,1)}) fusion(f32[16,128]{1,0:T(8,128)S(1)} %fusion.5, f32[1,16,128,512]{2,3,1,0:T(8,128)S(1)} %get-tuple-element.31, f32[16,128]{1,0:T(8,128)S(1)} %get-tuple-element.30, bf16[512,576]{1,0:T(8,128)(2,1)S(1)} %all_gather.3), kind=kOutput, calls=%fused_computation.18 | convolution fusion | flops 1078984704 | bytes 11026432 | tf_op jit(solution)/shard_map/shtj,sjd->sthd/dot_general | solution.py:55
  20.4 0.0 copy-done.1
  20.4 5.5 %copy.52 = f32[16,128,512]{2,0,1:T(8,128)} copy(f32[16,128,512]{1,2,0:T(8,128)} %get-tuple-element.32) | data formatting | bytes 8388608
  25.9 3.3 %multiply_reduce_fusion = f32[16,128]{0,1:T(8,128)S(1)} fusion(f32[16,128,512]{2,0,1:T(8,128)} %copy.52, bf16[1,128,16,512]{3,2,1,0:T(8,128)(2,1)} %param.11), kind=kLoop, calls=%fused_computation.6 | loop fusion | flops 3143680 | bytes 6299648
  29.3 0.1 copy.53
  29.3 0.0 copy-start.2
  29.3 0.0 copy-start.3
  29.3 6.8 %fusion.28 = f32[512,512]{1,0:T(8,128)} fusion(bf16[128,16,512]{2,1,0:T(8,128)(2,1)} %bitcast.147, f32[16,128]{1,0:T(8,128)S(1)} %fusion.5, f32[1,16,128,512]{2,3,1,0:T(8,128)} %copy-done.1, f32[16,128]{1,0:T(8,128)S(1)} %get-tuple-element.30), kind=kOutput, calls=%fused_computation.30 | convolution fusion | flops 1076887552 | bytes 7356416 | tf_op jit(solution)/shard_map/shtj,sthd->jd/dot_general | solution.py:76
  36.1 0.0 copy-done.2
  36.1 0.0 copy-done.3
  36.1 4.7 %fusion.1 = bf16[1,16,128,512]{2,3,1,0:T(8,128)(2,1)} fusion(f32[16,128]{1,0:T(8,128)S(1)} %copy.53, bf16[128,16,512]{2,1,0:T(8,128)(2,1)S(1)} %bitcast.148, f32[16,128]{1,0:T(8,128)S(1)} %fusion.5, f32[1,16,128,512]{2,3,1,0:T(8,128)S(1)} %copy-done.2, f32[16,128]{1,0:T(8,128)S(1)} %get-tuple-element.30, bf16[512,576]{1,0:T(8,128)(2,1)S(1)} %all_gather.3), kind=kOutput, calls=%fused_computation.2 | convolution fusion | flops 1078984704 | bytes 8937472 | tf_op jit(solution)/shard_map/sthd,sjd->shtj/dot_general | solution.py:61
  40.8 2.3 %fusion.69 = bf16[512,64]{0,1:T(8,128)(2,1)S(1)} fusion(bf16[1,16,128,512]{2,3,1,0:T(8,128)(2,1)} %fusion.1, bf16[1,16,64,128]{3,2,1,0:T(8,128)(2,1)S(1)} %copy-done.4), kind=kOutput, calls=%fused_computation.45 | convolution fusion | flops 134283264 | bytes 2424832 | tf_op jit(solution)/shard_map/shtj,shdt->jd/dot_general | solution.py:79
  43.2 4.4 %fusion.48 = bf16[512,512]{1,0:T(8,128)(2,1)S(1)} fusion(f32[512,512]{1,0:T(8,128)} %fusion.28, bf16[128,16,512]{2,1,0:T(8,128)(2,1)S(1)} %bitcast.146, bf16[1,16,128,512]{2,3,1,0:T(8,128)(2,1)} %fusion.1), kind=kOutput, calls=%fused_computation.34 | convolution fusion | flops 1074528256 | bytes 5767168 | tf_op jit(solution)/shard_map/shtj,sthd->jd/dot_general | solution.py:73
  47.6 0.1 copy.63
  47.7 0.8 fusion.82
  48.6 1.3 %collective-permute-start.2 = (bf16[128,576]{1,0:T(8,128)(2,1)}, bf16[128,576]{1,0:T(8,128)(2,1)}, u32[]{:S(2)}, u32[]{:S(2)}) collective-permute-start(bf16[128,576]{1,0:T(8,128)(2,1)} %get-tuple-element.29), channel_id=1, source_target_pairs={{24,0},{25,1},{26,2},{27,3},{28,4},{29,5},{30,6},{31,7}} | collective-permute-start | bytes 442376 | tf_op jit(solution)/shard_map/ppermute | solution.py:14
  49.9 1.3 %collective-permute-start.1 = (bf16[128,576]{1,0:T(8,128)(2,1)}, bf16[128,576]{1,0:T(8,128)(2,1)}, u32[]{:S(2)}, u32[]{:S(2)}) collective-permute-start(bf16[128,576]{1,0:T(8,128)(2,1)} %get-tuple-element.28), channel_id=1, source_target_pairs={{16,0},{24,8},{17,1},{25,9},{18,2},{26,10},{19,3},{27,11},{20,4},{... | collective-permute-start | bytes 442376 | tf_op jit(solution)/shard_map/ppermute | solution.py:14
  51.2 1.3 %collective-permute-start = (bf16[128,576]{1,0:T(8,128)(2,1)}, bf16[128,576]{1,0:T(8,128)(2,1)}, u32[]{:S(2)}, u32[]{:S(2)}) collective-permute-start(bf16[128,576]{1,0:T(8,128)(2,1)} %get-tuple-element.27), channel_id=1, source_target_pairs={{8,0},{16,8},{24,16},{9,1},{17,9},{25,17},{10,2},{18,10},{26,18},{... | collective-permute-start | bytes 442376 | tf_op jit(solution)/shard_map/ppermute | solution.py:14
  52.5 3.0 %collective-permute-done.2 = bf16[128,576]{1,0:T(8,128)(2,1)} collective-permute-done((bf16[128,576]{1,0:T(8,128)(2,1)}, bf16[128,576]{1,0:T(8,128)(2,1)}, u32[]{:S(2)}, u32[]{:S(2)}) %collective-permute-start.2) | collective-permute-done | bytes 147488 | tf_op jit(solution)/shard_map/ppermute | solution.py:14
  55.5 3.6 %collective-permute-done.1 = bf16[128,576]{1,0:T(8,128)(2,1)} collective-permute-done((bf16[128,576]{1,0:T(8,128)(2,1)}, bf16[128,576]{1,0:T(8,128)(2,1)}, u32[]{:S(2)}, u32[]{:S(2)}) %collective-permute-start.1) | collective-permute-done | bytes 147488 | tf_op jit(solution)/shard_map/ppermute | solution.py:14
  59.1 0.0 collective-permute-done
  59.1 1.2 %add_convert_fusion.3 = bf16[128,576]{1,0:T(8,128)(2,1)S(1)} fusion(bf16[128,576]{1,0:T(8,128)(2,1)} %collective-permute-done.2, bf16[128,576]{1,0:T(8,128)(2,1)} %collective-permute-done.1, bf16[128,576]{1,0:T(8,128)(2,1)} %collective-permute-done, s32[]{:T(128)S(6)} %select_n.22, bf16[4,128,512]{2,1,0:T(8,128)(2,1)S(1)} %bitcast.151, ...), kind=kLoop, calls=%fused_computation.54 | loop fusion | flops 958464 | bytes 1179653 | tf_op jit(solution)/shard_map/convert_element_type | solution.py:24
  60.3 1.6 %collective-permute-start.3 = (bf16[128,576]{1,0:T(8,128)(2,1)S(1)}, bf16[128,576]{1,0:T(8,128)(2,1)S(1)}, u32[]{:S(2)}, u32[]{:S(2)}) collective-permute-start(bf16[128,576]{1,0:T(8,128)(2,1)S(1)} %add_convert_fusion.3), channel_id=1, source_target_pairs={{0,1},{1,0},{2,3},{3,2},{4,5},{5,4},{6,7},{7,6},{8,9},{9,8},{10,11... | collective-permute-start | bytes 442376 | tf_op jit(solution)/shard_map/ppermute | solution.py:25
  61.9 4.9 %collective-permute-done.3 = bf16[128,576]{1,0:T(8,128)(2,1)S(1)} collective-permute-done((bf16[128,576]{1,0:T(8,128)(2,1)S(1)}, bf16[128,576]{1,0:T(8,128)(2,1)S(1)}, u32[]{:S(2)}, u32[]{:S(2)}) %collective-permute-start.3) | collective-permute-done | bytes 147488 | tf_op jit(solution)/shard_map/ppermute | solution.py:25
  66.8 1.6 %collective-permute-start.4 = (bf16[128,576]{1,0:T(8,128)(2,1)S(1)}, bf16[128,576]{1,0:T(8,128)(2,1)S(1)}, u32[]{:S(2)}, u32[]{:S(2)}) collective-permute-start(bf16[128,576]{1,0:T(8,128)(2,1)S(1)} %add_convert_fusion.2), channel_id=1, source_target_pairs={{0,2},{1,3},{2,0},{3,1},{4,6},{5,7},{6,4},{7,5},{8,10},{9,11},{10,... | collective-permute-start | bytes 442376 | tf_op jit(solution)/shard_map/ppermute | solution.py:25
  68.5 4.2 %fusion.25 = bf16[1,128,16,512]{1,3,2,0:T(8,128)(2,1)} fusion(bf16[1,16,128,512]{2,3,1,0:T(8,128)(2,1)} %fusion.1, bf16[512,576]{1,0:T(8,128)(2,1)S(1)} %all_gather.3), kind=kOutput, calls=%fused_computation.29 | convolution fusion | flops 1075838976 | bytes 4718592 | tf_op jit(solution)/shard_map/shtj,sjd->sthd/dot_general | solution.py:67
  72.7 4.5 %copy.41 = bf16[1,128,16,512]{3,2,1,0:T(8,128)(2,1)} copy(bf16[1,128,16,512]{1,3,2,0:T(8,128)(2,1)} %bitcast.149) | data formatting | bytes 4194304
  77.2 4.5 %copy.42 = bf16[1,128,16,512]{3,2,1,0:T(8,128)(2,1)} copy(bf16[1,128,16,512]{1,3,2,0:T(8,128)(2,1)} %fusion.25) | data formatting | bytes 4194304
  81.6 0.0 collective-permute-done.4
  81.7 2.6 %collective-permute-start.5 = (bf16[128,576]{1,0:T(8,128)(2,1)S(1)}, bf16[128,576]{1,0:T(8,128)(2,1)S(1)}, u32[]{:S(2)}, u32[]{:S(2)}) collective-permute-start(bf16[128,576]{1,0:T(8,128)(2,1)S(1)} %add_convert_fusion.1), channel_id=1, source_target_pairs={{0,4},{1,5},{2,6},{3,7},{4,0},{5,1},{6,2},{7,3},{8,12},{9,13},{10,... | collective-permute-start | bytes 442376 | tf_op jit(solution)/shard_map/ppermute | solution.py:25
  84.3 2.8 %fusion.60 = bf16[1,16,64,128]{3,2,1,0:T(8,128)(2,1)} fusion(bf16[1,16,128,512]{2,3,1,0:T(8,128)(2,1)} %fusion.1, bf16[512,576]{1,0:T(8,128)(2,1)S(1)} %all_gather.3), kind=kOutput, calls=%fused_computation.42 | convolution fusion | flops 134479872 | bytes 2490368 | tf_op jit(solution)/shard_map/shtj,sdj->shdt/dot_general | solution.py:71
  87.1 5.2 %collective-permute-done.5 = bf16[128,576]{1,0:T(8,128)(2,1)S(1)} collective-permute-done((bf16[128,576]{1,0:T(8,128)(2,1)S(1)}, bf16[128,576]{1,0:T(8,128)(2,1)S(1)}, u32[]{:S(2)}, u32[]{:S(2)}) %collective-permute-start.5) | collective-permute-done | bytes 147488 | tf_op jit(solution)/shard_map/ppermute | solution.py:25
  92.4 0.7 slice_bitcast_fusion.5
  93.0 0.7 copy.43
  (5 shorter events, 0.1 us)
Async XLA Ops:
  0.6 11.3 %copy-start = (bf16[1,128,16,512]{3,2,1,0:T(8,128)(2,1)S(1)}, bf16[1,128,16,512]{3,2,1,0:T(8,128)(2,1)}, u32[]{:S(2)}) copy-start(bf16[1,128,16,512]{3,2,1,0:T(8,128)(2,1)} %param.7) | copy-start | bytes 6291460
  12.0 2.8 %copy-start.4 = (bf16[1,16,64,128]{3,2,1,0:T(8,128)(2,1)S(1)}, bf16[1,16,64,128]{3,2,1,0:T(8,128)(2,1)}, u32[]{:S(2)}) copy-start(bf16[1,16,64,128]{3,2,1,0:T(8,128)(2,1)} %param.8) | copy-start | bytes 786436
  15.7 4.7 %copy-start.1 = (f32[1,16,128,512]{2,3,1,0:T(8,128)}, f32[1,16,128,512]{2,3,1,0:T(8,128)S(1)}, u32[]{:S(2)}) copy-start(f32[1,16,128,512]{2,3,1,0:T(8,128)S(1)} %get-tuple-element.31) | copy-start | bytes 12582916
  29.3 6.8 %copy-start.2 = (f32[1,16,128,512]{2,3,1,0:T(8,128)S(1)}, f32[1,16,128,512]{2,3,1,0:T(8,128)}, u32[]{:S(2)}) copy-start(f32[1,16,128,512]{2,3,1,0:T(8,128)} %copy-done.1) | copy-start | bytes 12582916
  29.3 6.8 %copy-start.3 = (bf16[1,128,16,512]{3,2,1,0:T(8,128)(2,1)S(1)}, bf16[1,128,16,512]{3,2,1,0:T(8,128)(2,1)}, u32[]{:S(2)}) copy-start(bf16[1,128,16,512]{3,2,1,0:T(8,128)(2,1)} %param.11) | copy-start | bytes 6291460
  48.6 6.9 %collective-permute-start.2 = (bf16[128,576]{1,0:T(8,128)(2,1)}, bf16[128,576]{1,0:T(8,128)(2,1)}, u32[]{:S(2)}, u32[]{:S(2)}) collective-permute-start(bf16[128,576]{1,0:T(8,128)(2,1)} %get-tuple-element.29), channel_id=1, source_target_pairs={{24,0},{25,1},{26,2},{27,3},{28,4},{29,5},{30,6},{31,7}} | collective-permute-start | bytes 442376 | tf_op jit(solution)/shard_map/ppermute | solution.py:14
  49.9 9.2 %collective-permute-start.1 = (bf16[128,576]{1,0:T(8,128)(2,1)}, bf16[128,576]{1,0:T(8,128)(2,1)}, u32[]{:S(2)}, u32[]{:S(2)}) collective-permute-start(bf16[128,576]{1,0:T(8,128)(2,1)} %get-tuple-element.28), channel_id=1, source_target_pairs={{16,0},{24,8},{17,1},{25,9},{18,2},{26,10},{19,3},{27,11},{20,4},{... | collective-permute-start | bytes 442376 | tf_op jit(solution)/shard_map/ppermute | solution.py:14
  51.2 7.9 %collective-permute-start = (bf16[128,576]{1,0:T(8,128)(2,1)}, bf16[128,576]{1,0:T(8,128)(2,1)}, u32[]{:S(2)}, u32[]{:S(2)}) collective-permute-start(bf16[128,576]{1,0:T(8,128)(2,1)} %get-tuple-element.27), channel_id=1, source_target_pairs={{8,0},{16,8},{24,16},{9,1},{17,9},{25,17},{10,2},{18,10},{26,18},{... | collective-permute-start | bytes 442376 | tf_op jit(solution)/shard_map/ppermute | solution.py:14
  60.3 6.5 %collective-permute-start.3 = (bf16[128,576]{1,0:T(8,128)(2,1)S(1)}, bf16[128,576]{1,0:T(8,128)(2,1)S(1)}, u32[]{:S(2)}, u32[]{:S(2)}) collective-permute-start(bf16[128,576]{1,0:T(8,128)(2,1)S(1)} %add_convert_fusion.3), channel_id=1, source_target_pairs={{0,1},{1,0},{2,3},{3,2},{4,5},{5,4},{6,7},{7,6},{8,9},{9,8},{10,11... | collective-permute-start | bytes 442376 | tf_op jit(solution)/shard_map/ppermute | solution.py:25
  66.8 14.8 %collective-permute-start.4 = (bf16[128,576]{1,0:T(8,128)(2,1)S(1)}, bf16[128,576]{1,0:T(8,128)(2,1)S(1)}, u32[]{:S(2)}, u32[]{:S(2)}) collective-permute-start(bf16[128,576]{1,0:T(8,128)(2,1)S(1)} %add_convert_fusion.2), channel_id=1, source_target_pairs={{0,2},{1,3},{2,0},{3,1},{4,6},{5,7},{6,4},{7,5},{8,10},{9,11},{10,... | collective-permute-start | bytes 442376 | tf_op jit(solution)/shard_map/ppermute | solution.py:25
  81.7 10.6 %collective-permute-start.5 = (bf16[128,576]{1,0:T(8,128)(2,1)S(1)}, bf16[128,576]{1,0:T(8,128)(2,1)S(1)}, u32[]{:S(2)}, u32[]{:S(2)}) collective-permute-start(bf16[128,576]{1,0:T(8,128)(2,1)S(1)} %add_convert_fusion.1), channel_id=1, source_target_pairs={{0,4},{1,5},{2,6},{3,7},{4,0},{5,1},{6,2},{7,3},{8,12},{9,13},{10,... | collective-permute-start | bytes 442376 | tf_op jit(solution)/shard_map/ppermute | solution.py:25
where the time goes:
time: 94.3 us; the launch traced here: 93.7 us
  matrix products  33.1 us (35%)
  local copies, waits for them, and re-layouts  17 us (18%)
  waiting for transfers between devices  16.8 us (18%)
  starting transfers between devices  9.74 us (10%)
  blocking collectives  9.33 us (10%)
  other arithmetic  7.04 us (7%)
    unnamed x15, local copies, waits for them, and re-layouts  16.2 us
    ppermute x3, waiting for transfers between devices, butterfly_sum_ep(): theirs = lax.ppermute(mine, 'ep', [(i, i ^ bit) for i in range(n_ep)])  10.1 us
    all_gather x1, blocking collectives, body(): whole_keys = lax.all_gather(local_keys, 'ctx', axis=0, tiled=True)  9.33 us
    dot_general x1, matrix products, body(): jnp.einsum('shtj,sthd->jd', rounded_weights, output_grad, preferred_eleme...  6.77 us
    ppermute x3, waiting for transfers between devices, causal_reduce_ctx(): lax.ppermute(sent, 'ctx', [(i, i - shift) for i in range(shift, n_ctx)])  6.64 us
    ppermute x3, starting transfers between devices, butterfly_sum_ep(): theirs = lax.ppermute(mine, 'ep', [(i, i ^ bit) for i in range(n_ep)])  5.87 us
    dot_general x1, matrix products, body(): jnp.einsum('sthd,sjd->shtj', output_grad, whole_latent, preferred_element...  4.71 us
    dot_general x1, matrix products, body(): jnp.einsum('shtj,sthd->jd', score_grad, query_latent, preferred_element_t...  4.44 us
  transfers between devices with their start and end apart: 6, of which 4 were waited for; matrix products, arithmetic and copies ran while one was open for 17% of the time, Pallas kernels for 0%

commit v1 on v0

--- a/solution.py
+++ b/solution.py
@@ -34,7 +34,21 @@
     block_len = query_latent.shape[1]
     kvr = key_latent.shape[2]
     local_keys = jnp.concatenate([key_latent[0], key_rope[0].T], axis=1)
-    whole_keys = lax.all_gather(local_keys, "ctx", axis=0, tiled=True)
+    ways, here_2, step = (lax.axis_size("ctx"), lax.axis_index("ctx"), local_keys.shape[0])
+    shape = [n * ways if d == 0 else n for d, n in enumerate(local_keys.shape)]
+    full = lax.dynamic_update_slice_in_dim(
+        jnp.zeros(shape, local_keys.dtype), local_keys, here_2 * step, axis=0
+    )
+    going_up = going_down = local_keys
+    for far in range(1, ways // 2 + 1):
+        going_up = lax.ppermute(going_up, "ctx", [(d, (d + 1) % ways) for d in range(ways)])
+        full = lax.dynamic_update_slice_in_dim(full, going_up, (here_2 - far) % ways * step, axis=0)
+        if 2 * far < ways:
+            going_down = lax.ppermute(going_down, "ctx", [(d, (d - 1) % ways) for d in range(ways)])
+            full = lax.dynamic_update_slice_in_dim(
+                full, going_down, (here_2 + far) % ways * step, axis=0
+            )
+    whole_keys = full
     whole_latent = whole_keys[None, :, :kvr]
     whole_rope = whole_keys[:, kvr:].T[None]
     length = whole_latent.shape[1]

time: 94.3 us -> 90.7 us (0.962)
  blocking collectives: 9.33 us -> 0 us
  waiting for transfers between devices: 16.8 us -> 23.4 us
  matrix products: 33.1 us -> 27.3 us
  starting transfers between devices: 9.74 us -> 13.9 us
    all_gather x1 -> x0, blocking collectives: 9.33 us -> none  [body(): whole_keys = lax.all_gather(local_keys, 'ctx', axis=0, tiled=True)]
    ppermute x0 -> x3, waiting for transfers between devices: none -> 5.89 us  [the longest x2 5.89 us: body(): lax.ppermute(going_up, 'ctx', [(d, (d + 1) % ways) for d in range(ways)])]
    ppermute x0 -> x3, starting transfers between devices: none -> 4.1 us  [the longest x2 2.11 us: body(): lax.ppermute(going_up, 'ctx', [(d, (d + 1) % ways) for d in range(ways)])]
    dot_general x1, matrix products: 4.44 us -> 2.57 us  [body(): jnp.einsum('shtj,sthd->jd', score_grad, query_latent, preferred_element_t...]
    dot_general x1, matrix products: 2.34 us -> 0.75 us  [body(): jnp.einsum('shtj,shdt->jd', score_grad, query_rope, preferred_element_typ...]
    dot_general x1, matrix products: 4.71 us -> 3.37 us  [body(): jnp.einsum('sthd,sjd->shtj', output_grad, whole_latent, preferred_element...]
    dot_general x1, matrix products: 6.77 us -> 5.8 us  [body(): jnp.einsum('shtj,sthd->jd', rounded_weights, output_grad, preferred_eleme...]
    unnamed x15 -> x17, local copies, waits for them, and re-layouts: 16.2 us -> 16.8 us
  transfers between devices with their start and end apart: 6 -> 9, of which waited for: 4 -> 6; matrix products, arithmetic and copies ran while one was open for 17% -> 18% of each run, Pallas kernels for 0% -> 0%
where the time goes in v1:
time: 90.7 us; the launch traced here: 90.2 us
  matrix products  27.3 us (30%)
  waiting for transfers between devices  23.4 us (26%)
  local copies, waits for them, and re-layouts  17.7 us (20%)
  starting transfers between devices  13.9 us (15%)
  other arithmetic  7.05 us (8%)
    unnamed x17, local copies, waits for them, and re-layouts  16.8 us
    ppermute x3, waiting for transfers between devices, butterfly_sum_ep(): theirs = lax.ppermute(mine, 'ep', [(i, i ^ bit) for i in range(n_ep)])  10.1 us
    ppermute x3, waiting for transfers between devices, causal_reduce_ctx(): lax.ppermute(sent, 'ctx', [(i, i - shift) for i in range(shift, n_ctx)])  7.35 us
    ppermute x3, starting transfers between devices, butterfly_sum_ep(): theirs = lax.ppermute(mine, 'ep', [(i, i ^ bit) for i in range(n_ep)])  5.9 us
    ppermute x2, waiting for transfers between devices, body(): lax.ppermute(going_up, 'ctx', [(d, (d + 1) % ways) for d in range(ways)])  5.89 us
    dot_general x1, matrix products, body(): jnp.einsum('shtj,sthd->jd', rounded_weights, output_grad, preferred_eleme...  5.8 us
    dot_general x1, matrix products, body(): jnp.einsum('shtj,sjd->sthd', score_grad, whole_latent, preferred_element_...  4.19 us
    dot_general x1, matrix products, body(): jnp.einsum('shtj,sjd->sthd', rounded_weights, whole_latent, preferred_ele...  4.12 us
  transfers between devices with their start and end apart: 9, of which 6 were waited for; matrix products, arithmetic and copies ran while one was open for 18% of the time, Pallas kernels for 0%

profile of v1, /device:TPU:0, one launch (start us, length us, event | category | flops | bytes accessed | tf_op | source)
XLA Modules:
  0.0 90.2 jit_solution(563572583066952554)
XLA Ops:
  0.6 0.0 copy-start
  0.6 1.0 %copy.27 = bf16[1,64,128]{1,2,0:T(8,128)(2,1)S(1)} copy(bf16[1,64,128]{2,1,0:T(8,128)(2,1)} %param.10) | data formatting | bytes 32768 | tf_op args[3]
  1.6 0.1 broadcast_in_dim.33
  1.7 0.9 %pad_maximum_fusion = (bf16[128,576]{1,0:T(8,128)(2,1)S(1)}, bf16[512,576]{1,0:T(8,128)(2,1)S(1)}) fusion(bf16[128,64]{1,0:T(8,128)(2,1)S(1)} %bitcast.155, bf16[128,512]{1,0:T(8,128)(2,1)} %bitcast.154, bf16[512,576]{1,0:T(8,128)(2,1)S(1)} %broadcast_in_dim.33, s32[]{:T(128)S(6)} %select_n.37), kind=kLoop, calls=%fused_computation.70 | loop fusion | flops 294912 | bytes 491524 | tf_op jit(solution)/shard_map/concatenate | solution.py:36
  2.6 0.5 collective-permute-start
  3.1 2.0 %collective-permute-start.1 = (bf16[128,576]{1,0:T(8,128)(2,1)S(1)}, bf16[128,576]{1,0:T(8,128)(2,1)S(1)}, u32[]{:S(2)}, u32[]{:S(2)}) collective-permute-start(bf16[128,576]{1,0:T(8,128)(2,1)S(1)} %get-tuple-element.30), channel_id=1, source_target_pairs={{0,24},{8,0},{16,8},{24,16},{1,25},{9,1},{17,9},{25,17},{2,26},{10... | collective-permute-start | bytes 442376 | tf_op jit(solution)/shard_map/ppermute | solution.py:47
  5.1 0.1 iota_compare_fusion
  5.3 2.8 %collective-permute-done = bf16[128,576]{1,0:T(8,128)(2,1)S(1)} collective-permute-done((bf16[128,576]{1,0:T(8,128)(2,1)S(1)}, bf16[128,576]{1,0:T(8,128)(2,1)S(1)}, u32[]{:S(2)}, u32[]{:S(2)}) %collective-permute-start) | collective-permute-done | bytes 147488 | tf_op jit(solution)/shard_map/ppermute | solution.py:44
  8.1 1.6 %collective-permute-start.2 = (bf16[128,576]{1,0:T(8,128)(2,1)S(1)}, bf16[128,576]{1,0:T(8,128)(2,1)S(1)}, u32[]{:S(2)}, u32[]{:S(2)}) collective-permute-start(bf16[128,576]{1,0:T(8,128)(2,1)S(1)} %collective-permute-done), channel_id=1, source_target_pairs={{0,8},{8,16},{16,24},{24,0},{1,9},{9,17},{17,25},{25,1},{2,10},{10... | collective-permute-start | bytes 442376 | tf_op jit(solution)/shard_map/ppermute | solution.py:44
  9.7 0.0 collective-permute-done.1
  9.8 3.1 %collective-permute-done.2 = bf16[128,576]{1,0:T(8,128)(2,1)S(1)} collective-permute-done((bf16[128,576]{1,0:T(8,128)(2,1)S(1)}, bf16[128,576]{1,0:T(8,128)(2,1)S(1)}, u32[]{:S(2)}, u32[]{:S(2)}) %collective-permute-start.2) | collective-permute-done | bytes 147488 | tf_op jit(solution)/shard_map/ppermute | solution.py:44
  12.8 0.0 copy-done
  12.9 0.0 copy-start.5
  12.9 2.8 %fusion.23 = f32[512,128,16]{1,0,2:T(8,128)S(1)} fusion(bf16[128,16,512]{2,1,0:T(8,128)(2,1)S(1)} %bitcast.145, bf16[512,576]{1,0:T(8,128)(2,1)S(1)} %constant_dynamic-update-slice_fusion), kind=kOutput, calls=%fused_computation.27 | convolution fusion | flops 1073741824 | bytes 6815744 | tf_op jit(solution)/shard_map/sthd,sjd->shtj/dot_general | solution.py:58
  15.7 0.0 copy-done.5
  15.7 0.9 fusion.88
  16.6 0.0 copy-start.1
  16.6 0.6 fusion.5
  17.2 4.1 %bitcast_convert_fusion = (f32[16,128,512]{1,2,0:T(8,128)}, bf16[512,16,128]{2,0,1:T(8,128)(2,1)}) fusion(f32[16,128]{1,0:T(8,128)S(1)} %fusion.5, f32[1,16,128,512]{2,3,1,0:T(8,128)S(1)} %get-tuple-element.33, f32[16,128]{1,0:T(8,128)S(1)} %get-tuple-element.32, bf16[512,576]{1,0:T(8,128)(2,1)S(1)} %constant_dynamic-update-slice_fusion), kind=kOutput, calls=%fused_computation.18 | convolution fusion | flops 1078984704 | bytes 11026432 | tf_op jit(solution)/shard_map/shtj,sjd->sthd/dot_general | solution.py:69
  21.3 0.0 copy-done.1
  21.3 5.5 %copy.52 = f32[16,128,512]{2,0,1:T(8,128)} copy(f32[16,128,512]{1,2,0:T(8,128)} %get-tuple-element.34) | data formatting | bytes 8388608
  26.8 3.3 %multiply_reduce_fusion = f32[16,128]{0,1:T(8,128)S(1)} fusion(f32[16,128,512]{2,0,1:T(8,128)} %copy.52, bf16[1,128,16,512]{3,2,1,0:T(8,128)(2,1)} %param.11), kind=kLoop, calls=%fused_computation.6 | loop fusion | flops 3143680 | bytes 6299648
  30.2 0.1 copy.53
  30.2 0.0 copy-start.2
  30.2 0.0 copy-start.4
  30.2 5.8 %fusion.28 = f32[512,512]{1,0:T(8,128)S(1)} fusion(bf16[128,16,512]{2,1,0:T(8,128)(2,1)} %bitcast.147, f32[16,128]{1,0:T(8,128)S(1)} %fusion.5, f32[1,16,128,512]{2,3,1,0:T(8,128)} %copy-done.1, f32[16,128]{1,0:T(8,128)S(1)} %get-tuple-element.32), kind=kOutput, calls=%fused_computation.30 | convolution fusion | flops 1076887552 | bytes 7356416 | tf_op jit(solution)/shard_map/shtj,sthd->jd/dot_general | solution.py:90
  36.0 0.0 copy-done.2
  36.0 0.0 copy-done.4
  36.0 3.4 %fusion.1 = bf16[1,16,128,512]{2,3,1,0:T(8,128)(2,1)S(1)} fusion(f32[16,128]{1,0:T(8,128)S(1)} %copy.53, bf16[128,16,512]{2,1,0:T(8,128)(2,1)S(1)} %bitcast.148, f32[16,128]{1,0:T(8,128)S(1)} %fusion.5, f32[1,16,128,512]{2,3,1,0:T(8,128)S(1)} %copy-done.2, f32[16,128]{1,0:T(8,128)S(1)} %get-tuple-element.32, ...), kind=kOutput, calls=%fused_computation.2 | convolution fusion | flops 1078984704 | bytes 8937472 | tf_op jit(solution)/shard_map/sthd,sjd->shtj/dot_general | solution.py:75
  39.4 0.0 copy-start.3
  39.4 0.8 fusion.69
  40.2 0.6 copy-done.3
  40.8 2.6 %fusion.48 = bf16[512,512]{1,0:T(8,128)(2,1)S(1)} fusion(f32[512,512]{1,0:T(8,128)S(1)} %fusion.28, bf16[128,16,512]{2,1,0:T(8,128)(2,1)S(1)} %bitcast.146, bf16[1,16,128,512]{2,3,1,0:T(8,128)(2,1)S(1)} %fusion.1), kind=kOutput, calls=%fused_computation.34 | convolution fusion | flops 1074528256 | bytes 5767168 | tf_op jit(solution)/shard_map/shtj,sthd->jd/dot_general | solution.py:87
  43.3 0.1 copy.63
  43.5 0.8 fusion.82
  44.3 1.3 %collective-permute-start.5 = (bf16[128,576]{1,0:T(8,128)(2,1)}, bf16[128,576]{1,0:T(8,128)(2,1)}, u32[]{:S(2)}, u32[]{:S(2)}) collective-permute-start(bf16[128,576]{1,0:T(8,128)(2,1)} %get-tuple-element.29), channel_id=1, source_target_pairs={{24,0},{25,1},{26,2},{27,3},{28,4},{29,5},{30,6},{31,7}} | collective-permute-start | bytes 442376 | tf_op jit(solution)/shard_map/ppermute | solution.py:14
  45.6 1.3 %collective-permute-start.4 = (bf16[128,576]{1,0:T(8,128)(2,1)}, bf16[128,576]{1,0:T(8,128)(2,1)}, u32[]{:S(2)}, u32[]{:S(2)}) collective-permute-start(bf16[128,576]{1,0:T(8,128)(2,1)} %get-tuple-element.28), channel_id=1, source_target_pairs={{16,0},{24,8},{17,1},{25,9},{18,2},{26,10},{19,3},{27,11},{20,4},{... | collective-permute-start | bytes 442376 | tf_op jit(solution)/shard_map/ppermute | solution.py:14
  46.9 1.3 %collective-permute-start.3 = (bf16[128,576]{1,0:T(8,128)(2,1)}, bf16[128,576]{1,0:T(8,128)(2,1)}, u32[]{:S(2)}, u32[]{:S(2)}) collective-permute-start(bf16[128,576]{1,0:T(8,128)(2,1)} %get-tuple-element.27), channel_id=1, source_target_pairs={{8,0},{16,8},{24,16},{9,1},{17,9},{25,17},{10,2},{18,10},{26,18},{... | collective-permute-start | bytes 442376 | tf_op jit(solution)/shard_map/ppermute | solution.py:14
  48.2 3.0 %collective-permute-done.5 = bf16[128,576]{1,0:T(8,128)(2,1)} collective-permute-done((bf16[128,576]{1,0:T(8,128)(2,1)}, bf16[128,576]{1,0:T(8,128)(2,1)}, u32[]{:S(2)}, u32[]{:S(2)}) %collective-permute-start.5) | collective-permute-done | bytes 147488 | tf_op jit(solution)/shard_map/ppermute | solution.py:14
  51.2 4.3 %collective-permute-done.4 = bf16[128,576]{1,0:T(8,128)(2,1)} collective-permute-done((bf16[128,576]{1,0:T(8,128)(2,1)}, bf16[128,576]{1,0:T(8,128)(2,1)}, u32[]{:S(2)}, u32[]{:S(2)}) %collective-permute-start.4) | collective-permute-done | bytes 147488 | tf_op jit(solution)/shard_map/ppermute | solution.py:14
  55.5 0.0 collective-permute-done.3
  55.5 1.2 %add_convert_fusion.3 = bf16[128,576]{1,0:T(8,128)(2,1)S(1)} fusion(bf16[128,576]{1,0:T(8,128)(2,1)} %collective-permute-done.5, bf16[128,576]{1,0:T(8,128)(2,1)} %collective-permute-done.4, bf16[128,576]{1,0:T(8,128)(2,1)} %collective-permute-done.3, s32[]{:T(128)S(6)} %select_n.55, bf16[4,128,512]{2,1,0:T(8,128)(2,1)S(1)} %bitcast.151, ...), kind=kLoop, calls=%fused_computation.54 | loop fusion | flops 958464 | bytes 1179653 | tf_op jit(solution)/shard_map/convert_element_type | solution.py:24
  56.7 1.6 %collective-permute-start.6 = (bf16[128,576]{1,0:T(8,128)(2,1)S(1)}, bf16[128,576]{1,0:T(8,128)(2,1)S(1)}, u32[]{:S(2)}, u32[]{:S(2)}) collective-permute-start(bf16[128,576]{1,0:T(8,128)(2,1)S(1)} %add_convert_fusion.3), channel_id=1, source_target_pairs={{0,1},{1,0},{2,3},{3,2},{4,5},{5,4},{6,7},{7,6},{8,9},{9,8},{10,11... | collective-permute-start | bytes 442376 | tf_op jit(solution)/shard_map/ppermute | solution.py:25
  58.3 5.0 %collective-permute-done.6 = bf16[128,576]{1,0:T(8,128)(2,1)S(1)} collective-permute-done((bf16[128,576]{1,0:T(8,128)(2,1)S(1)}, bf16[128,576]{1,0:T(8,128)(2,1)S(1)}, u32[]{:S(2)}, u32[]{:S(2)}) %collective-permute-start.6) | collective-permute-done | bytes 147488 | tf_op jit(solution)/shard_map/ppermute | solution.py:25
  63.3 1.6 %collective-permute-start.7 = (bf16[128,576]{1,0:T(8,128)(2,1)S(1)}, bf16[128,576]{1,0:T(8,128)(2,1)S(1)}, u32[]{:S(2)}, u32[]{:S(2)}) collective-permute-start(bf16[128,576]{1,0:T(8,128)(2,1)S(1)} %add_convert_fusion.2), channel_id=1, source_target_pairs={{0,2},{1,3},{2,0},{3,1},{4,6},{5,7},{6,4},{7,5},{8,10},{9,11},{10,... | collective-permute-start | bytes 442376 | tf_op jit(solution)/shard_map/ppermute | solution.py:25
  64.9 4.2 %fusion.25 = bf16[1,128,16,512]{1,3,2,0:T(8,128)(2,1)} fusion(bf16[1,16,128,512]{2,3,1,0:T(8,128)(2,1)} %copy-done.3, bf16[512,576]{1,0:T(8,128)(2,1)S(1)} %constant_dynamic-update-slice_fusion), kind=kOutput, calls=%fused_computation.29 | convolution fusion | flops 1075838976 | bytes 4718592 | tf_op jit(solution)/shard_map/shtj,sjd->sthd/dot_general | solution.py:81
  69.1 4.5 %copy.41 = bf16[1,128,16,512]{3,2,1,0:T(8,128)(2,1)} copy(bf16[1,128,16,512]{1,3,2,0:T(8,128)(2,1)} %bitcast.149) | data formatting | bytes 4194304
  73.6 4.5 %copy.42 = bf16[1,128,16,512]{3,2,1,0:T(8,128)(2,1)} copy(bf16[1,128,16,512]{1,3,2,0:T(8,128)(2,1)} %fusion.25) | data formatting | bytes 4194304
  78.1 0.0 collective-permute-done.7
  78.2 2.7 %collective-permute-start.8 = (bf16[128,576]{1,0:T(8,128)(2,1)S(1)}, bf16[128,576]{1,0:T(8,128)(2,1)S(1)}, u32[]{:S(2)}, u32[]{:S(2)}) collective-permute-start(bf16[128,576]{1,0:T(8,128)(2,1)S(1)} %add_convert_fusion.1), channel_id=1, source_target_pairs={{0,4},{1,5},{2,6},{3,7},{4,0},{5,1},{6,2},{7,3},{8,12},{9,13},{10,... | collective-permute-start | bytes 442376 | tf_op jit(solution)/shard_map/ppermute | solution.py:25
  80.8 2.8 %fusion.60 = bf16[1,16,64,128]{3,2,1,0:T(8,128)(2,1)} fusion(bf16[1,16,128,512]{2,3,1,0:T(8,128)(2,1)} %copy-done.3, bf16[512,576]{1,0:T(8,128)(2,1)S(1)} %constant_dynamic-update-slice_fusion), kind=kOutput, calls=%fused_computation.42 | convolution fusion | flops 134479872 | bytes 2490368 | tf_op jit(solution)/shard_map/shtj,sdj->shdt/dot_general | solution.py:85
  83.6 5.2 %collective-permute-done.8 = bf16[128,576]{1,0:T(8,128)(2,1)S(1)} collective-permute-done((bf16[128,576]{1,0:T(8,128)(2,1)S(1)}, bf16[128,576]{1,0:T(8,128)(2,1)S(1)}, u32[]{:S(2)}, u32[]{:S(2)}) %collective-permute-start.8) | collective-permute-done | bytes 147488 | tf_op jit(solution)/shard_map/ppermute | solution.py:25
  88.8 0.7 slice_bitcast_fusion.5
  89.5 0.7 copy.43
  (8 shorter events, 0.2 us)
Async XLA Ops:
  0.6 12.2 %copy-start = (bf16[1,128,16,512]{3,2,1,0:T(8,128)(2,1)S(1)}, bf16[1,128,16,512]{3,2,1,0:T(8,128)(2,1)}, u32[]{:S(2)}) copy-start(bf16[1,128,16,512]{3,2,1,0:T(8,128)(2,1)} %param.7) | copy-start | bytes 6291460
  2.6 5.4 %collective-permute-start = (bf16[128,576]{1,0:T(8,128)(2,1)S(1)}, bf16[128,576]{1,0:T(8,128)(2,1)S(1)}, u32[]{:S(2)}, u32[]{:S(2)}) collective-permute-start(bf16[128,576]{1,0:T(8,128)(2,1)S(1)} %get-tuple-element.30), channel_id=1, source_target_pairs={{0,8},{8,16},{16,24},{24,0},{1,9},{9,17},{17,25},{25,1},{2,10},{10... | collective-permute-start | bytes 442376 | tf_op jit(solution)/shard_map/ppermute | solution.py:44
  3.1 6.6 %collective-permute-start.1 = (bf16[128,576]{1,0:T(8,128)(2,1)S(1)}, bf16[128,576]{1,0:T(8,128)(2,1)S(1)}, u32[]{:S(2)}, u32[]{:S(2)}) collective-permute-start(bf16[128,576]{1,0:T(8,128)(2,1)S(1)} %get-tuple-element.30), channel_id=1, source_target_pairs={{0,24},{8,0},{16,8},{24,16},{1,25},{9,1},{17,9},{25,17},{2,26},{10... | collective-permute-start | bytes 442376 | tf_op jit(solution)/shard_map/ppermute | solution.py:47
  8.1 4.7 %collective-permute-start.2 = (bf16[128,576]{1,0:T(8,128)(2,1)S(1)}, bf16[128,576]{1,0:T(8,128)(2,1)S(1)}, u32[]{:S(2)}, u32[]{:S(2)}) collective-permute-start(bf16[128,576]{1,0:T(8,128)(2,1)S(1)} %collective-permute-done), channel_id=1, source_target_pairs={{0,8},{8,16},{16,24},{24,0},{1,9},{9,17},{17,25},{25,1},{2,10},{10... | collective-permute-start | bytes 442376 | tf_op jit(solution)/shard_map/ppermute | solution.py:44
  12.9 2.8 %copy-start.5 = (bf16[1,16,64,128]{3,2,1,0:T(8,128)(2,1)S(1)}, bf16[1,16,64,128]{3,2,1,0:T(8,128)(2,1)}, u32[]{:S(2)}) copy-start(bf16[1,16,64,128]{3,2,1,0:T(8,128)(2,1)} %param.8) | copy-start | bytes 786436
  16.6 4.7 %copy-start.1 = (f32[1,16,128,512]{2,3,1,0:T(8,128)}, f32[1,16,128,512]{2,3,1,0:T(8,128)S(1)}, u32[]{:S(2)}) copy-start(f32[1,16,128,512]{2,3,1,0:T(8,128)S(1)} %get-tuple-element.33) | copy-start | bytes 12582916
  30.2 5.8 %copy-start.2 = (f32[1,16,128,512]{2,3,1,0:T(8,128)S(1)}, f32[1,16,128,512]{2,3,1,0:T(8,128)}, u32[]{:S(2)}) copy-start(f32[1,16,128,512]{2,3,1,0:T(8,128)} %copy-done.1) | copy-start | bytes 12582916
  30.2 5.8 %copy-start.4 = (bf16[1,128,16,512]{3,2,1,0:T(8,128)(2,1)S(1)}, bf16[1,128,16,512]{3,2,1,0:T(8,128)(2,1)}, u32[]{:S(2)}) copy-start(bf16[1,128,16,512]{3,2,1,0:T(8,128)(2,1)} %param.11) | copy-start | bytes 6291460
  39.4 1.3 %copy-start.3 = (bf16[1,16,128,512]{2,3,1,0:T(8,128)(2,1)}, bf16[1,16,128,512]{2,3,1,0:T(8,128)(2,1)S(1)}, u32[]{:S(2)}) copy-start(bf16[1,16,128,512]{2,3,1,0:T(8,128)(2,1)S(1)} %fusion.1) | copy-start | bytes 6291460
  44.3 6.9 %collective-permute-start.5 = (bf16[128,576]{1,0:T(8,128)(2,1)}, bf16[128,576]{1,0:T(8,128)(2,1)}, u32[]{:S(2)}, u32[]{:S(2)}) collective-permute-start(bf16[128,576]{1,0:T(8,128)(2,1)} %get-tuple-element.29), channel_id=1, source_target_pairs={{24,0},{25,1},{26,2},{27,3},{28,4},{29,5},{30,6},{31,7}} | collective-permute-start | bytes 442376 | tf_op jit(solution)/shard_map/ppermute | solution.py:14
  45.6 10.0 %collective-permute-start.4 = (bf16[128,576]{1,0:T(8,128)(2,1)}, bf16[128,576]{1,0:T(8,128)(2,1)}, u32[]{:S(2)}, u32[]{:S(2)}) collective-permute-start(bf16[128,576]{1,0:T(8,128)(2,1)} %get-tuple-element.28), channel_id=1, source_target_pairs={{16,0},{24,8},{17,1},{25,9},{18,2},{26,10},{19,3},{27,11},{20,4},{... | collective-permute-start | bytes 442376 | tf_op jit(solution)/shard_map/ppermute | solution.py:14
  46.9 8.7 %collective-permute-start.3 = (bf16[128,576]{1,0:T(8,128)(2,1)}, bf16[128,576]{1,0:T(8,128)(2,1)}, u32[]{:S(2)}, u32[]{:S(2)}) collective-permute-start(bf16[128,576]{1,0:T(8,128)(2,1)} %get-tuple-element.27), channel_id=1, source_target_pairs={{8,0},{16,8},{24,16},{9,1},{17,9},{25,17},{10,2},{18,10},{26,18},{... | collective-permute-start | bytes 442376 | tf_op jit(solution)/shard_map/ppermute | solution.py:14
  56.7 6.6 %collective-permute-start.6 = (bf16[128,576]{1,0:T(8,128)(2,1)S(1)}, bf16[128,576]{1,0:T(8,128)(2,1)S(1)}, u32[]{:S(2)}, u32[]{:S(2)}) collective-permute-start(bf16[128,576]{1,0:T(8,128)(2,1)S(1)} %add_convert_fusion.3), channel_id=1, source_target_pairs={{0,1},{1,0},{2,3},{3,2},{4,5},{5,4},{6,7},{7,6},{8,9},{9,8},{10,11... | collective-permute-start | bytes 442376 | tf_op jit(solution)/shard_map/ppermute | solution.py:25
  63.3 14.8 %collective-permute-start.7 = (bf16[128,576]{1,0:T(8,128)(2,1)S(1)}, bf16[128,576]{1,0:T(8,128)(2,1)S(1)}, u32[]{:S(2)}, u32[]{:S(2)}) collective-permute-start(bf16[128,576]{1,0:T(8,128)(2,1)S(1)} %add_convert_fusion.2), channel_id=1, source_target_pairs={{0,2},{1,3},{2,0},{3,1},{4,6},{5,7},{6,4},{7,5},{8,10},{9,11},{10,... | collective-permute-start | bytes 442376 | tf_op jit(solution)/shard_map/ppermute | solution.py:25
  78.2 10.6 %collective-permute-start.8 = (bf16[128,576]{1,0:T(8,128)(2,1)S(1)}, bf16[128,576]{1,0:T(8,128)(2,1)S(1)}, u32[]{:S(2)}, u32[]{:S(2)}) collective-permute-start(bf16[128,576]{1,0:T(8,128)(2,1)S(1)} %add_convert_fusion.1), channel_id=1, source_target_pairs={{0,4},{1,5},{2,6},{3,7},{4,0},{5,1},{6,2},{7,3},{8,12},{9,13},{10,... | collective-permute-start | bytes 442376 | tf_op jit(solution)/shard_map/ppermute | solution.py:25
